TPU v7x, 32 devices: a whole 2x2x4 slice. The times are simulated.
32 devices in a mesh: seq: 8 (over y, x, core), tp: 4 (over z).
Axes of the slice: x: 2, y: 2, z: 4, core: 2. Of those that a mesh axis runs over, the one named last changes fastest.
Arguments:
- hidden: bfloat16 [4096, 2560], P('seq', 'tp'), may hold values from -6 to 6
- norm_gain: float32 [2560], replicated, may hold values from 0.25 to 1.75
- query_weight: float32 [2560, 4096], P('seq', 'tp'), may hold values from -0.125 to 0.125
- key_weight: float32 [2560, 1024], P('seq', 'tp'), may hold values from -0.125 to 0.125
- value_weight: float32 [2560, 1024], P('seq', 'tp'), may hold values from -0.125 to 0.125
- query_gain: float32 [128], replicated, may hold values from 0.5 to 8
- key_gain: float32 [128], replicated, may hold values from 0.5 to 8
- lengths: int32 [8], replicated, may hold values from 1 to 2048, 4096 in all
- page_table: int32 [32], replicated, may hold values from 0 to 31, each once
Outputs:
- attention: bfloat16 [4096, 4096], P('seq', 'tp')
- key_cache: bfloat16 [32, 8, 128, 128], P('seq', 'tp')
- value_cache: bfloat16 [32, 8, 128, 128], P('seq', 'tp')
Inputs may be any that keep to these rules, and one draw needn't show every extreme that they name: 8 positive lengths summing to 4096; the longest is exactly 2048. `page_table`: every page is named by exactly one block.
All inputs are finite; a program needn't handle non-finite values.
Results may differ from a plain program's by a relative error of at most 0.0085.
The roundings to bfloat16 on the way count: a program that leaves them out, or rounds other values in their place, can miss the bound.
Values may be sent and summed in bfloat16 or wider, within the bound.
No kernel may reach another device: no remote copies, remote signals or barrier semaphores. Data moves between devices by JAX's collectives and lax.ppermute only.
A program may use at most 128 MiB of HBM per device.

v0:
```python
import math
from functools import partial

import jax
import jax.numpy as jnp
from jax import lax
from jax.sharding import Mesh, PartitionSpec as P
from jax.experimental import pallas as pl
from jax.experimental.pallas import tpu as pltpu

PAGE = 128


epsilon = 1e-06
excluded = -1e30


def segment_of(slot_index, prompt_ends):
    return jnp.sum((slot_index[..., None] >= prompt_ends).astype(jnp.int32), axis=-1)


def position_of(slot_index, prompt_ends, lengths):
    segment_id = segment_of(slot_index, prompt_ends)
    prompt_starts = prompt_ends - lengths
    labels = jnp.arange(lengths.shape[0], dtype=jnp.int32)
    picked = jnp.sum(jnp.where(segment_id[..., None] == labels, prompt_starts, 0), axis=-1)
    return (segment_id, slot_index - picked)


def head_norm(vectors, gain):
    mean_sq = jnp.mean(vectors * vectors, axis=-1, keepdims=True)
    return vectors * lax.rsqrt(mean_sq + epsilon) * gain


def rotate(vectors, position):
    head_dim = vectors.shape[-1]
    half_dim = head_dim // 2
    frequency = 1000000.0 ** (-(jnp.arange(half_dim, dtype=jnp.float32) * 2.0 / head_dim))
    angles = position.astype(jnp.float32)[:, None] * frequency[None, :]
    cosine = jnp.cos(angles)[:, None, :]
    sine_part = jnp.sin(angles)[:, None, :]
    front = vectors[..., :half_dim]
    back_half = vectors[..., half_dim:]
    return jnp.concatenate(
        [front * cosine - back_half * sine_part, back_half * cosine + front * sine_part], axis=-1
    )


def attend(
    query_block,
    query_slots,
    query_segments,
    key_piece,
    value_piece,
    key_slots,
    key_segments,
    kv_heads,
    group_size,
    head_dim,
    running,
):
    running_max, denominator, accumulator = running
    half_rows = query_block.shape[0]
    key_count = key_piece.shape[0]
    scores = jnp.einsum(
        "qkgd,nkd->kgqn",
        query_block.reshape(half_rows, kv_heads, group_size, head_dim),
        key_piece.reshape(key_count, kv_heads, head_dim),
        preferred_element_type=jnp.float32,
    ) * head_dim ** (-0.5)
    allowed = (key_segments[None, :] == query_segments[:, None]) & (
        key_slots[None, :] <= query_slots[:, None]
    )
    masked = jnp.where(allowed, scores, excluded)
    new_max = jnp.maximum(running_max, jnp.max(masked, axis=-1))
    weights = jnp.where(allowed, jnp.exp(scores - new_max[..., None]), 0.0)
    denominator = jnp.sum(weights, axis=-1)
    probs = weights.astype(jnp.bfloat16)
    accumulator = jnp.einsum(
        "kgqn,nkd->kgqd",
        probs,
        value_piece.reshape(key_count, kv_heads, head_dim),
        preferred_element_type=jnp.float32,
    )
    return (new_max, denominator, accumulator)


def flash_kernel(group_size, block_q, block_k, head_dim, chips, rank_rows, meta_ref, q_ref, k_ref, v_ref, rs_ref, o_ref, m_sc, l_sc, acc_sc):
    i = pl.program_id(1)
    r0 = meta_ref[3 * i]
    s_first = meta_ref[3 * i + 1]
    s_last = meta_ref[3 * i + 2]
    rows = group_size * block_q
    q = q_ref[...]
    qs = jnp.concatenate([q[:, g * head_dim : (g + 1) * head_dim] for g in range(group_size)], axis=0)
    rstart = jnp.concatenate([rs_ref[...]] * group_size, axis=0)
    row_slot = r0 + lax.broadcasted_iota(jnp.int32, (group_size, block_q, 1), 1).reshape(rows, 1)
    m_sc[...] = jnp.full(m_sc.shape, excluded, jnp.float32)
    l_sc[...] = jnp.zeros(l_sc.shape, jnp.float32)
    acc_sc[...] = jnp.zeros(acc_sc.shape, jnp.float32)
    scale = head_dim ** (-0.5) * math.log2(math.e)

    def update(kb, masked):
        first = kb * block_k
        rank = first // rank_rows
        stored = pl.multiple_of(first, block_k)
        k = k_ref[pl.ds(stored, block_k), :]
        v = v_ref[pl.ds(stored, block_k), :]
        s = lax.dot_general(qs, k, (((1,), (1,)), ((), ())), preferred_element_type=jnp.float32)
        if masked:
            cols = first + lax.broadcasted_iota(jnp.int32, (rows, block_k), 1)
            allowed = (cols >= rstart) & (cols <= row_slot)
            s_max = jnp.max(jnp.where(allowed, s, excluded), axis=1, keepdims=True)
        else:
            s_max = jnp.max(s, axis=1, keepdims=True)
        m_prev = m_sc[...]
        m_next = jnp.maximum(m_prev, s_max)
        alpha = jnp.exp2((m_prev - m_next) * scale)
        p = jnp.exp2((s - m_next[:, :1]) * scale)
        if masked:
            p = jnp.where(allowed, p, 0.0)
        l_sc[...] = alpha * l_sc[...] + jnp.sum(p, axis=1, keepdims=True)
        pv = jnp.dot(p.astype(jnp.bfloat16), v, preferred_element_type=jnp.float32)
        acc_sc[...] = acc_sc[...] * alpha + pv
        m_sc[...] = m_next

    def body(kb, carry):
        lo = kb * block_k
        full = (lo >= s_last) & (lo + block_k - 1 <= r0)

        @pl.when(full)
        def _():
            update(kb, False)

        @pl.when(jnp.logical_not(full))
        def _():
            update(kb, True)

        return carry

    lax.fori_loop(s_first // block_k, (r0 + block_q - 1) // block_k + 1, body, 0)
    res = acc_sc[...] / l_sc[...]
    o_ref[...] = jnp.concatenate(
        [res[g * block_q : (g + 1) * block_q] for g in range(group_size)], axis=1
    ).astype(o_ref.dtype)


def flash(meta, queries, both, row_start, kv_heads, group_size, head_dim, block_q, block_k, chips):
    row_count = queries.shape[0]
    key_count = both.shape[0]
    n_qb = row_count // block_q
    rows = group_size * block_q
    kernel = partial(flash_kernel, group_size, block_q, block_k, head_dim, chips, row_count)
    grid_spec = pltpu.PrefetchScalarGridSpec(
        num_scalar_prefetch=1,
        grid=(kv_heads, n_qb),
        in_specs=[
            pl.BlockSpec((block_q, group_size * head_dim), lambda h, i, meta: (i, h)),
            pl.BlockSpec((key_count, head_dim), lambda h, i, meta: (0, h)),
            pl.BlockSpec((key_count, head_dim), lambda h, i, meta: (0, kv_heads + h)),
            pl.BlockSpec((block_q, 1), lambda h, i, meta: (i, 0)),
        ],
        out_specs=pl.BlockSpec((block_q, group_size * head_dim), lambda h, i, meta: (i, h)),
        scratch_shapes=[
            pltpu.VMEM((rows, head_dim), jnp.float32),
            pltpu.VMEM((rows, head_dim), jnp.float32),
            pltpu.VMEM((rows, head_dim), jnp.float32),
        ],
    )
    flops = 4 * kv_heads * rows * n_qb * 1536 * head_dim
    return pl.pallas_call(
        kernel,
        grid_spec=grid_spec,
        out_shape=jax.ShapeDtypeStruct(queries.shape, queries.dtype),
        compiler_params=pltpu.CompilerParams(dimension_semantics=("arbitrary", "arbitrary")),
        cost_estimate=pl.CostEstimate(
            flops=flops, transcendentals=flops // (4 * head_dim), bytes_accessed=2 * queries.size * 2 + both.size * 2
        ),
    )(meta, queries, both, both, row_start)


def shards(
    chips,
    tp_size,
    hidden,
    norm_gain,
    query_weight,
    key_weight,
    value_weight,
    query_gain,
    key_gain,
    lengths,
    page_table,
):
    row_count = hidden.shape[0]
    head_dim = query_gain.shape[0]
    query_cols = query_weight.shape[1]
    key_cols = key_weight.shape[1]
    kv_heads = key_cols // head_dim
    group_size = query_cols // key_cols
    seq_rank = lax.axis_index("seq")
    prompt_ends = jnp.cumsum(lengths)
    tp_rank = lax.axis_index("tp")
    pieces = [hidden]
    for shift in range(1, tp_size):
        pairs = [(i, (i + shift) % tp_size) for i in range(tp_size)]
        pieces.append(lax.ppermute(hidden, "tp", pairs))
    gathered = jnp.concatenate(
        [lax.select_n((tp_rank - u) % tp_size, *pieces) for u in range(tp_size)], axis=1
    )
    widened = gathered.astype(jnp.float32)
    normed = (
        widened
        * lax.rsqrt(jnp.mean(widened * widened, axis=-1, keepdims=True) + epsilon)
        * norm_gain
    ).astype(jnp.bfloat16)
    server_block = jnp.concatenate([query_weight, key_weight, value_weight], axis=1).astype(
        jnp.bfloat16
    )
    full_block = lax.all_gather(server_block, "seq", axis=0, tiled=True)
    normed_perm = normed
    projected_kv = jnp.dot(normed_perm, full_block[:, query_cols:], preferred_element_type=jnp.float32)
    slot_index = seq_rank * row_count + jnp.arange(row_count, dtype=jnp.int32)
    segment_id, position = position_of(slot_index, prompt_ends, lengths)
    key_rows = rotate(
        head_norm(projected_kv[:, :key_cols].reshape(row_count, kv_heads, head_dim), key_gain),
        position,
    )
    key_rows = key_rows.reshape(row_count, key_cols).astype(jnp.bfloat16)
    values = projected_kv[:, key_cols:].astype(jnp.bfloat16)
    local_kv = jnp.concatenate([key_rows, values], axis=1)
    both_piece = lax.all_gather(local_kv, "seq", axis=0, tiled=True)
    projected_q = jnp.dot(normed_perm, full_block[:, :query_cols], preferred_element_type=jnp.float32)
    queries = rotate(
        head_norm(projected_q.reshape(row_count, query_cols // head_dim, head_dim), query_gain),
        position,
    )
    queries = queries.reshape(row_count, query_cols).astype(jnp.bfloat16)
    block_q = 128
    block_k = 512
    row_start = slot_index - position
    firsts = row_start[::block_q]
    lasts = row_start[block_q - 1 :: block_q]
    meta = jnp.stack([slot_index[::block_q], firsts, lasts], axis=1).reshape(-1).astype(jnp.int32)
    attention = flash(
        meta, queries, both_piece, row_start.reshape(row_count, 1).astype(jnp.int32),
        kv_heads, group_size, head_dim, block_q, block_k, chips,
    )
    pages_dev = row_count // PAGE
    owned_pages = seq_rank * pages_dev + jnp.arange(pages_dev, dtype=jnp.int32)
    page_count = page_table.shape[0]
    source_block = jnp.sum(
        jnp.where(
            page_table[None, :] == owned_pages[:, None],
            jnp.arange(page_count, dtype=jnp.int32)[None, :],
            0,
        ),
        axis=1,
    )
    stored = source_block * PAGE
    pages = jnp.stack([lax.dynamic_slice_in_dim(both_piece, stored[p], PAGE, 0) for p in range(pages_dev)])
    key_cache = pages[:, :, :key_cols].reshape(pages_dev, PAGE, kv_heads, head_dim).transpose(0, 2, 1, 3)
    value_cache = pages[:, :, key_cols:].reshape(pages_dev, PAGE, kv_heads, head_dim).transpose(0, 2, 1, 3)
    return (attention, key_cache, value_cache)


def solution(mesh):
    seq_size = mesh.shape["seq"]
    tp_size = mesh.shape["tp"]
    chips = seq_size // 2
    return jax.shard_map(
        partial(shards, chips, tp_size),
        mesh=mesh,
        in_specs=(
            P("seq", "tp"),
            P(),
            P("seq", "tp"),
            P("seq", "tp"),
            P("seq", "tp"),
            P(),
            P(),
            P(),
            P(),
        ),
        out_specs=(P("seq", "tp"), P("seq", "tp", None, None), P("seq", "tp", None, None)),
        check_vma=False,
    )
```

profile of v0, /device:TPU:4, one launch (start us, length us, event | category | flops | bytes accessed | tf_op | source)
XLA Modules:
  0.0 159.5 jit_solution(14281594908395345751)
XLA Ops:
  7.2 0.0 all-gather.3.cloned.1.call-start
  7.2 1.0 convert.25
  8.2 0.0 copy-start
  8.2 1.1 convert.26
  9.3 0.0 copy-start.6
  9.3 1.4 convert.24
  10.7 1.0 pad_maximum_fusion.2
  11.7 0.0 all-gather.3.cloned.1.call-update
  11.7 0.0 all-gather.5.cloned.1.call-start
  11.8 1.6 %collective-permute-start = (bf16[512,640]{1,0:T(8,128)(2,1)S(1)}, bf16[512,640]{1,0:T(8,128)(2,1)S(1)}, u32[]{:S(2)}, u32[]{:S(2)}) collective-permute-start(bf16[512,640]{1,0:T(8,128)(2,1)S(1)} %copy-done), channel_id=1, source_target_pairs={{0,1},{1,2},{2,3},{3,0},{4,5},{5,6},{6,7},{7,4},{8,9},{9,10},{10,1... | collective-permute-start | bytes 1966088 | tf_op jit(solution)/shard_map/ppermute | solution.py:207
  13.4 2.6 %collective-permute-start.1 = (bf16[512,640]{1,0:T(8,128)(2,1)S(1)}, bf16[512,640]{1,0:T(8,128)(2,1)S(1)}, u32[]{:S(2)}, u32[]{:S(2)}) collective-permute-start(bf16[512,640]{1,0:T(8,128)(2,1)S(1)} %copy-done), channel_id=1, source_target_pairs={{0,2},{1,3},{2,0},{3,1},{4,6},{5,7},{6,4},{7,5},{8,10},{9,11},{10,... | collective-permute-start | bytes 1966088 | tf_op jit(solution)/shard_map/ppermute | solution.py:207
  16.0 1.3 collective-permute-start.2
  17.4 0.2 reduce-window.8
  17.6 0.1 convert_reduce_fusion
  17.7 0.1 select_reduce_fusion
  17.8 0.5 multiply_cosine_fusion
  18.3 13.1 %collective-permute-done = bf16[512,640]{1,0:T(8,128)(2,1)S(1)} collective-permute-done((bf16[512,640]{1,0:T(8,128)(2,1)S(1)}, bf16[512,640]{1,0:T(8,128)(2,1)S(1)}, u32[]{:S(2)}, u32[]{:S(2)}) %collective-permute-start) | collective-permute-done | bytes 655392 | tf_op jit(solution)/shard_map/ppermute | solution.py:207
  31.4 27.0 %collective-permute-done.1 = bf16[512,640]{1,0:T(8,128)(2,1)S(1)} collective-permute-done((bf16[512,640]{1,0:T(8,128)(2,1)S(1)}, bf16[512,640]{1,0:T(8,128)(2,1)S(1)}, u32[]{:S(2)}, u32[]{:S(2)}) %collective-permute-start.1) | collective-permute-done | bytes 655392 | tf_op jit(solution)/shard_map/ppermute | solution.py:207
  58.4 0.0 copy-done.1
  58.4 0.9 copy-done.2
  59.3 0.0 collective-permute-done.2
  59.3 1.9 %select_select_fusion.3 = (bf16[512,640]{1,0:T(8,128)(2,1)S(1)}, bf16[512,640]{1,0:T(8,128)(2,1)S(1)}, bf16[512,640]{1,0:T(8,128)(2,1)S(1)}, bf16[512,640]{1,0:T(8,128)(2,1)S(1)}) fusion(bf16[512,640]{1,0:T(8,128)(2,1)} %copy-done.2, bf16[512,640]{1,0:T(8,128)(2,1)} %collective-permute-done.2, bf16[512,640]{1,0:T(8,128)(2,1)S(1)} %copy-done, ...), kind=kLoop, calls=%fused_computation.21 | loop fusion | flops 3932160 | bytes 5242892 | tf_op jit(solution)/shard_map/select_n | solution.py:209
  61.2 0.0 copy-start.5
  61.2 0.7 fusion
  62.0 0.0 copy-start.3
  62.0 2.8 %all-gather.3.cloned.1.call-done = bf16[2560,1536]{1,0:T(8,128)(2,1)} async-done(((bf16[320,1536]{1,0:T(8,128)(2,1)}), bf16[2560,1536]{1,0:T(8,128)(2,1)}) %all-gather.3.cloned.1.call-update) | async-done | bytes 7864336 | tf_op jit(solution)/shard_map/all_gather | solution.py:220
  64.8 3.4 %fusion.5 = f32[512,512]{0,1:T(8,128)S(1)} fusion(bf16[2560,1536]{1,0:T(8,128)(2,1)} %all-gather.3.cloned.1.call-done, f32[2560]{0:T(1024)S(1)} %copy-done.5, f32[512]{0:T(512)S(1)} %add_rsqrt_fusion.2, bf16[512,640]{1,0:T(8,128)(2,1)S(1)} %get-tuple-element.28, bf16[512,640]{1,0:T(8,128)(2,1)S(1)} %get-tuple-element.29, ...), kind=kOutput, calls=%fused_computation.7 | convolution fusion | flops 1356595200 | bytes 6303744 | tf_op jit(solution)/shard_map/dot_general | solution.py:222
  68.2 0.1 multiply_reduce_fusion.1
  68.3 0.0 copy-done.3
  68.3 0.0 copy-start.7
  68.4 0.1 multiply_multiply_fusion.1
  68.5 0.1 subtract_convert_fusion.1
  68.6 0.8 copy.72
  69.4 0.1 copy.73
  69.6 1.8 %pad_maximum_fusion.3 = bf16[512,512]{1,0:T(8,128)(2,1)} fusion(bf16[512,256]{1,0:T(8,128)(2,1)S(1)} %copy.73, bf16[512,256]{1,0:T(8,128)(2,1)} %copy.72), kind=kLoop, calls=%fused_computation.22 | loop fusion | flops 1048576 | bytes 1048576 | tf_op jit(solution)/shard_map/concatenate | solution.py:231
  71.4 0.0 all-gather.5.cloned.1.call-update
  71.4 0.2 select_reduce_fusion.1
  71.6 0.6 fusion.13
  77.2 0.1 slice.52
  77.3 0.1 slice.54
  77.3 0.1 slice.53
  77.4 0.1 copy.63
  77.6 0.1 copy.64
  77.7 0.1 copy.60
  77.8 0.7 reshape.147.meta_ref
  78.5 0.9 copy.67.rs_ref
  81.8 5.4 %fusion.7 = f32[64,8,8,128]{3,1,2,0:T(8,128)S(1)} fusion(bf16[2560,1536]{1,0:T(8,128)(2,1)} %all-gather.3.cloned.1.call-done, f32[2560]{0:T(1024)} %param.10, f32[512]{0:T(512)S(1)} %add_rsqrt_fusion.2, bf16[512,640]{1,0:T(8,128)(2,1)S(1)} %get-tuple-element.28, bf16[512,640]{1,0:T(8,128)(2,1)S(1)} %get-tuple-element.29, ...), kind=kOutput, calls=%fused_computation.14 | convolution fusion | flops 2698772480 | bytes 9975808 | tf_op jit(solution)/shard_map/dot_general | solution.py:233
  87.2 0.0 copy-start.4
  87.3 0.5 copy.74
  87.7 0.6 multiply_reduce_fusion
  88.3 0.1 copy.61
  88.5 0.1 copy.62
  88.6 0.9 multiply_multiply_fusion
  89.5 0.9 subtract_convert_fusion
  90.3 0.6 pad_maximum_fusion.1
  90.9 1.2 copy.77
  92.2 26.2 %all-gather.5.cloned.1.call-done.k_ref.v_ref = bf16[4096,512]{1,0:T(8,128)(2,1)} async-done(((bf16[512,512]{1,0:T(8,128)(2,1)}), bf16[4096,512]{1,0:T(8,128)(2,1)}) %all-gather.5.cloned.1.call-update) | async-done | bytes 4194320 | tf_op jit(solution)/shard_map/all_gather | solution.py:232
  118.3 1.2 dynamic-slice_bitcast_fusion.3
  119.6 0.1 pad_maximum_fusion.4
  119.7 0.2 copy.69
  119.9 0.9 copy.71
  120.7 0.2 copy.68
  120.9 0.9 copy.70
  121.7 30.9 %shard_map.112 = bf16[512,1024]{1,0:T(8,128)(2,1)} custom-call(s32[12]{0:T(128)} %reshape.147.meta_ref, bf16[512,1024]{1,0:T(8,128)(2,1)} %bitcast.39, bf16[4096,512]{1,0:T(8,128)(2,1)} %all-gather.5.cloned.1.call-done.k_ref.v_ref, bf16[4096,512]{1,0:T(8,128)(2,1)} %all-gather.5.cloned.1.call-done.k_ref.v_ref, s32[512,1]{1,0:T(8,128)} %copy.67.rs_ref), custom_call_target="tpu_custom_call" | custom-call | flops 3221225472 | bytes 6291456 | tf_op jit(solution)/shard_map/pallas_call | solution.py:171
  (20 shorter events, 0.2 us)
Async XLA Ops:
  7.2 57.7 %all-gather.3.cloned.1.call-start = ((), (), s32[]{:S(2)}) async-start(), calls=%async_computation | async-start | bytes 8847360 | tf_op jit(solution)/shard_map/all_gather | solution.py:220
  8.2 3.6 %copy-start = (bf16[512,640]{1,0:T(8,128)(2,1)S(1)}, bf16[512,640]{1,0:T(8,128)(2,1)}, u32[]{:S(2)}) copy-start(bf16[512,640]{1,0:T(8,128)(2,1)} %param.9) | copy-start | bytes 1966084
  9.3 8.1 %copy-start.6 = (s32[8]{0:T(128)S(1)}, s32[8]{0:T(128)}, u32[]{:S(2)}) copy-start(s32[8]{0:T(128)} %param.16) | copy-start | bytes 100
  11.7 106.6 %all-gather.5.cloned.1.call-start = ((), (), s32[]{:S(2)}) async-start(), calls=%async_computation.1 | async-start | bytes 4718592 | tf_op jit(solution)/shard_map/all_gather | solution.py:232
  11.8 19.6 %collective-permute-start = (bf16[512,640]{1,0:T(8,128)(2,1)S(1)}, bf16[512,640]{1,0:T(8,128)(2,1)S(1)}, u32[]{:S(2)}, u32[]{:S(2)}) collective-permute-start(bf16[512,640]{1,0:T(8,128)(2,1)S(1)} %copy-done), channel_id=1, source_target_pairs={{0,1},{1,2},{2,3},{3,0},{4,5},{5,6},{6,7},{7,4},{8,9},{9,10},{10,1... | collective-permute-start | bytes 1966088 | tf_op jit(solution)/shard_map/ppermute | solution.py:207
  13.4 45.0 %collective-permute-start.1 = (bf16[512,640]{1,0:T(8,128)(2,1)S(1)}, bf16[512,640]{1,0:T(8,128)(2,1)S(1)}, u32[]{:S(2)}, u32[]{:S(2)}) collective-permute-start(bf16[512,640]{1,0:T(8,128)(2,1)S(1)} %copy-done), channel_id=1, source_target_pairs={{0,2},{1,3},{2,0},{3,1},{4,6},{5,7},{6,4},{7,5},{8,10},{9,11},{10,... | collective-permute-start | bytes 1966088 | tf_op jit(solution)/shard_map/ppermute | solution.py:207
  16.0 43.3 %collective-permute-start.2 = (bf16[512,640]{1,0:T(8,128)(2,1)S(1)}, bf16[512,640]{1,0:T(8,128)(2,1)}, u32[]{:S(2)}, u32[]{:S(2)}) collective-permute-start(bf16[512,640]{1,0:T(8,128)(2,1)S(1)} %copy-done), channel_id=1, source_target_pairs={{0,3},{1,0},{2,1},{3,2},{4,7},{5,4},{6,5},{7,6},{8,11},{9,8},{10,9... | collective-permute-start | bytes 1966088 | tf_op jit(solution)/shard_map/ppermute | solution.py:207
  31.4 27.0 %copy-start.1 = (bf16[512,640]{1,0:T(8,128)(2,1)}, bf16[512,640]{1,0:T(8,128)(2,1)S(1)}, u32[]{:S(2)}) copy-start(bf16[512,640]{1,0:T(8,128)(2,1)S(1)} %collective-permute-done) | copy-start | bytes 1966084
  58.4 0.9 copy-start.2
  61.2 3.6 %copy-start.5 = (f32[2560]{0:T(1024)S(1)}, f32[2560]{0:T(1024)}, u32[]{:S(2)}) copy-start(f32[2560]{0:T(1024)} %param.10) | copy-start | bytes 30724
  62.0 6.4 %copy-start.3 = (f32[128]{0:T(128)S(1)}, f32[128]{0:T(128)}, u32[]{:S(2)}) copy-start(f32[128]{0:T(128)} %param.15) | copy-start | bytes 1540
  68.3 3.1 %copy-start.7 = (s32[32]{0:T(128)S(1)}, s32[32]{0:T(128)}, u32[]{:S(2)}) copy-start(s32[32]{0:T(128)} %param.17) | copy-start | bytes 388
  87.2 1.4 copy-start.4
Sparse Core Ops, SparseCore 0:
  11.9 52.9 all-gather.2
  71.5 46.7 all-gather.4
where the time goes:
time: 160 us
  waiting for transfers between devices  69.1 us (43%)
  Pallas kernels  30.9 us (19%)
  between operations  21.8 us (14%)
  other arithmetic  13.3 us (8%)
  local copies, waits for them, and re-layouts  9.93 us (6%)
  matrix products  8.8 us (6%)
  starting transfers between devices  5.65 us (4%)
    ppermute x3, waiting for transfers between devices, shards(): pieces.append(lax.ppermute(hidden, 'tp', pairs))  40.1 us
    pallas_call x1, Pallas kernels, flash(): pl.pallas_call(kernel, grid_spec=grid_spec, out_shape=jax.ShapeDtypeStruc...  30.9 us
    all_gather x1, waiting for transfers between devices, shards(): both_piece = lax.all_gather(local_kv, 'seq', axis=0, tiled=True)  26.2 us
    ppermute x3, starting transfers between devices, shards(): pieces.append(lax.ppermute(hidden, 'tp', pairs))  5.57 us
    dot_general x1, matrix products, shards(): jnp.dot(normed_perm, full_block[:, :query_cols], preferred_element_type=j...  5.41 us
    another operation x6, other arithmetic  4.59 us
    unnamed x21, local copies, waits for them, and re-layouts  4.48 us
    dot_general x1, matrix products, shards(): jnp.dot(normed_perm, full_block[:, query_cols:], preferred_element_type=j...  3.39 us
  transfers between devices with their start and end apart: 5, of which 4 were waited for; matrix products, arithmetic and copies ran while one was open for 11% of the time, Pallas kernels for 0%

commit v1 on v0

--- a/solution.py
+++ b/solution.py
@@ -85,7 +85,7 @@
     return (new_max, denominator, accumulator)
 
 
-def flash_kernel(group_size, block_q, block_k, head_dim, chips, rank_rows, meta_ref, q_ref, k_ref, v_ref, rs_ref, o_ref, m_sc, l_sc, acc_sc):
+def flash_kernel(group_size, block_q, block_k, head_dim, chips, rank_rows, meta_ref, where_ref, q_ref, k_ref, v_ref, rs_ref, o_ref, m_sc, l_sc, acc_sc):
     i = pl.program_id(1)
     r0 = meta_ref[3 * i]
     s_first = meta_ref[3 * i + 1]
@@ -102,8 +102,7 @@
 
     def update(kb, masked):
         first = kb * block_k
-        rank = first // rank_rows
-        stored = pl.multiple_of(first, block_k)
+        stored = pl.multiple_of(where_ref[first // rank_rows] * rank_rows + first % rank_rows, block_k)
         k = k_ref[pl.ds(stored, block_k), :]
         v = v_ref[pl.ds(stored, block_k), :]
         s = lax.dot_general(qs, k, (((1,), (1,)), ((), ())), preferred_element_type=jnp.float32)
@@ -145,22 +144,22 @@
     ).astype(o_ref.dtype)
 
 
-def flash(meta, queries, both, row_start, kv_heads, group_size, head_dim, block_q, block_k, chips):
+def flash(meta, where, queries, both, row_start, kv_heads, group_size, head_dim, block_q, block_k, chips):
     row_count = queries.shape[0]
     key_count = both.shape[0]
     n_qb = row_count // block_q
     rows = group_size * block_q
     kernel = partial(flash_kernel, group_size, block_q, block_k, head_dim, chips, row_count)
     grid_spec = pltpu.PrefetchScalarGridSpec(
-        num_scalar_prefetch=1,
+        num_scalar_prefetch=2,
         grid=(kv_heads, n_qb),
         in_specs=[
-            pl.BlockSpec((block_q, group_size * head_dim), lambda h, i, meta: (i, h)),
-            pl.BlockSpec((key_count, head_dim), lambda h, i, meta: (0, h)),
-            pl.BlockSpec((key_count, head_dim), lambda h, i, meta: (0, kv_heads + h)),
-            pl.BlockSpec((block_q, 1), lambda h, i, meta: (i, 0)),
+            pl.BlockSpec((block_q, group_size * head_dim), lambda h, i, meta, where: (i, h)),
+            pl.BlockSpec((key_count, head_dim), lambda h, i, meta, where: (0, h)),
+            pl.BlockSpec((key_count, head_dim), lambda h, i, meta, where: (0, kv_heads + h)),
+            pl.BlockSpec((block_q, 1), lambda h, i, meta, where: (i, 0)),
         ],
-        out_specs=pl.BlockSpec((block_q, group_size * head_dim), lambda h, i, meta: (i, h)),
+        out_specs=pl.BlockSpec((block_q, group_size * head_dim), lambda h, i, meta, where: (i, h)),
         scratch_shapes=[
             pltpu.VMEM((rows, head_dim), jnp.float32),
             pltpu.VMEM((rows, head_dim), jnp.float32),
@@ -176,7 +175,37 @@
         cost_estimate=pl.CostEstimate(
             flops=flops, transcendentals=flops // (4 * head_dim), bytes_accessed=2 * queries.size * 2 + both.size * 2
         ),
-    )(meta, queries, both, both, row_start)
+    )(meta, where, queries, both, both, row_start)
+
+
+def gather_rows(x, chips):
+    seq_size = 2 * chips
+    me = lax.axis_index("seq")
+    if chips != 4:
+        return lax.all_gather(x, "seq", axis=0, tiled=True), jnp.arange(seq_size, dtype=jnp.int32)
+
+    def swap(value, bit):
+        return lax.ppermute(value, "seq", [(i, i ^ bit) for i in range(seq_size)])
+
+    from_partner = swap(x, 1)
+    from_x = swap(x, 2)
+    from_y = swap(x, 4)
+    forward = jnp.where(me % 2 == 0, from_y, from_x)
+    from_diagonal = lax.ppermute(
+        forward, "seq", [(i, i ^ 2) if i % 2 == 0 else (i, i ^ 4) for i in range(seq_size)]
+    )
+    by_mask = [
+        x,
+        from_partner,
+        from_x,
+        swap(from_x, 1),
+        from_y,
+        swap(from_y, 1),
+        from_diagonal,
+        swap(from_diagonal, 1),
+    ]
+    where = jnp.bitwise_xor(jnp.arange(seq_size, dtype=jnp.int32), me)
+    return jnp.concatenate(by_mask, axis=0), where
 
 
 def shards(
@@ -229,7 +258,7 @@
     key_rows = key_rows.reshape(row_count, key_cols).astype(jnp.bfloat16)
     values = projected_kv[:, key_cols:].astype(jnp.bfloat16)
     local_kv = jnp.concatenate([key_rows, values], axis=1)
-    both_piece = lax.all_gather(local_kv, "seq", axis=0, tiled=True)
+    both_piece, where = gather_rows(local_kv, chips)
     projected_q = jnp.dot(normed_perm, full_block[:, :query_cols], preferred_element_type=jnp.float32)
     queries = rotate(
         head_norm(projected_q.reshape(row_count, query_cols // head_dim, head_dim), query_gain),
@@ -243,7 +272,7 @@
     lasts = row_start[block_q - 1 :: block_q]
     meta = jnp.stack([slot_index[::block_q], firsts, lasts], axis=1).reshape(-1).astype(jnp.int32)
     attention = flash(
-        meta, queries, both_piece, row_start.reshape(row_count, 1).astype(jnp.int32),
+        meta, where, queries, both_piece, row_start.reshape(row_count, 1).astype(jnp.int32),
         kv_heads, group_size, head_dim, block_q, block_k, chips,
     )
     pages_dev = row_count // PAGE
@@ -257,7 +286,7 @@
         ),
         axis=1,
     )
-    stored = source_block * PAGE
+    stored = where[source_block // pages_dev] * row_count + (source_block % pages_dev) * PAGE
     pages = jnp.stack([lax.dynamic_slice_in_dim(both_piece, stored[p], PAGE, 0) for p in range(pages_dev)])
     key_cache = pages[:, :, :key_cols].reshape(pages_dev, PAGE, kv_heads, head_dim).transpose(0, 2, 1, 3)
     value_cache = pages[:, :, key_cols:].reshape(pages_dev, PAGE, kv_heads, head_dim).transpose(0, 2, 1, 3)

time: 160 us -> 158 us (0.988)
  the two profiles are of different devices: /device:TPU:4 before, /device:TPU:15 now
where the time goes in v1:
time: 158 us; the launch traced here: 161 us
  waiting for transfers between devices  50.5 us (32%)
  Pallas kernels  38.1 us (24%)
  between operations  21.9 us (14%)
  local copies, waits for them, and re-layouts  17.4 us (11%)
  other arithmetic  14.8 us (9%)
  starting transfers between devices  9.26 us (6%)
  matrix products  8.9 us (6%)
    ppermute x3, waiting for transfers between devices, shards(): pieces.append(lax.ppermute(hidden, 'tp', pairs))  41.5 us
    pallas_call x1, Pallas kernels, flash(): pl.pallas_call(kernel, grid_spec=grid_spec, out_shape=jax.ShapeDtypeStruc...  38.1 us
    unnamed x32, local copies, waits for them, and re-layouts  9.77 us
    dot_general x1, matrix products, shards(): jnp.dot(normed_perm, full_block[:, :query_cols], preferred_element_type=j...  5.44 us
    ppermute x6, starting transfers between devices, swap(): return lax.ppermute(value, 'seq', [(i, i ^ bit) for i in range(seq_size)])  5.17 us
    ppermute x6, waiting for transfers between devices, swap(): return lax.ppermute(value, 'seq', [(i, i ^ bit) for i in range(seq_size)])  4.74 us
    another operation x6, other arithmetic  4.57 us
    ppermute x1, waiting for transfers between devices, gather_rows(): lax.ppermute(forward, 'seq', [(i, i ^ 2) if i % 2 == 0 else (i, i ^ 4) fo...  4.15 us
  transfers between devices with their start and end apart: 11, of which 5 were waited for; matrix products, arithmetic and copies ran while one was open for 15% of the time, Pallas kernels for 0%

profile of v1, /device:TPU:15, one launch (start us, length us, event | category | flops | bytes accessed | tf_op | source)
XLA Modules:
  0.0 160.8 jit_solution(2838064381349596545)
XLA Ops:
  7.2 1.0 convert.25
  8.3 1.0 convert.26
  9.3 1.4 convert.24
  10.7 1.0 pad_maximum_fusion.2
  11.7 1.3 collective-permute-start
  13.1 1.1 collective-permute-start.1
  14.2 1.4 collective-permute-start.2
  15.6 0.2 reduce-window.8
  15.8 0.1 slice.52
  15.9 0.1 convert_reduce_fusion
  15.9 0.1 select_reduce_fusion
  16.0 0.1 slice.54
  16.1 0.1 slice.53
  16.3 0.2 select_reduce_fusion.1
  16.5 0.6 gather_fusion
  17.1 0.7 fusion.17
  22.8 0.1 copy.60
  22.9 0.6 reshape.205.meta_ref
  23.5 0.5 multiply_cosine_fusion
  24.0 0.8 copy.63
  24.9 0.8 copy.64
  25.7 0.9 copy.67.rs_ref
  29.1 39.5 %collective-permute-done.1 = bf16[512,640]{1,0:T(8,128)(2,1)S(1)} collective-permute-done((bf16[512,640]{1,0:T(8,128)(2,1)S(1)}, bf16[512,640]{1,0:T(8,128)(2,1)S(1)}, u32[]{:S(2)}, u32[]{:S(2)}) %collective-permute-start.1) | collective-permute-done | bytes 655392 | tf_op jit(solution)/shard_map/ppermute | solution.py:236
  68.6 0.9 copy-done.5
  69.6 2.0 %collective-permute-done.2 = bf16[512,640]{1,0:T(8,128)(2,1)} collective-permute-done((bf16[512,640]{1,0:T(8,128)(2,1)S(1)}, bf16[512,640]{1,0:T(8,128)(2,1)}, u32[]{:S(2)}, u32[]{:S(2)}) %collective-permute-start.2) | collective-permute-done | bytes 655392 | tf_op jit(solution)/shard_map/ppermute | solution.py:236
  71.6 1.9 %select_select_fusion.3 = (bf16[512,640]{1,0:T(8,128)(2,1)S(1)}, bf16[512,640]{1,0:T(8,128)(2,1)S(1)}, bf16[512,640]{1,0:T(8,128)(2,1)S(1)}, bf16[512,640]{1,0:T(8,128)(2,1)S(1)}) fusion(bf16[512,640]{1,0:T(8,128)(2,1)} %copy-done.5, bf16[512,640]{1,0:T(8,128)(2,1)} %collective-permute-done.2, bf16[512,640]{1,0:T(8,128)(2,1)S(1)} %copy-done.3, ...), kind=kLoop, calls=%fused_computation.22 | loop fusion | flops 3932160 | bytes 5242892 | tf_op jit(solution)/shard_map/select_n | solution.py:238
  73.5 0.9 fusion
  74.5 3.5 %fusion.5 = f32[512,512]{0,1:T(8,128)S(1)} fusion(bf16[2560,1536]{1,0:T(8,128)(2,1)} %all-gather.2.cloned.1.call-done, f32[2560]{0:T(1024)S(1)} %copy-done.8, f32[512]{0:T(512)S(1)} %add_rsqrt_fusion.2, bf16[512,640]{1,0:T(8,128)(2,1)S(1)} %get-tuple-element.28, bf16[512,640]{1,0:T(8,128)(2,1)S(1)} %get-tuple-element.29, ...), kind=kOutput, calls=%fused_computation.8 | convolution fusion | flops 1356595200 | bytes 6303744 | tf_op jit(solution)/shard_map/dot_general | solution.py:251
  78.1 0.1 multiply_multiply_fusion.1
  78.2 0.1 subtract_convert_fusion.1
  78.3 0.1 copy.72
  78.4 0.1 copy.73
  78.6 1.1 pad_maximum_fusion.3
  79.7 0.3 collective-permute-start.4
  79.9 0.8 collective-permute-start.3
  80.7 0.2 collective-permute-start.6
  80.9 5.4 %fusion.7 = f32[64,8,8,128]{3,1,2,0:T(8,128)S(1)} fusion(bf16[2560,1536]{1,0:T(8,128)(2,1)} %all-gather.2.cloned.1.call-done, f32[2560]{0:T(1024)S(1)} %copy-done.8, f32[512]{0:T(512)S(1)} %add_rsqrt_fusion.2, bf16[512,640]{1,0:T(8,128)(2,1)S(1)} %get-tuple-element.28, bf16[512,640]{1,0:T(8,128)(2,1)S(1)} %get-tuple-element.29, ...), kind=kOutput, calls=%fused_computation.15 | convolution fusion | flops 2698772480 | bytes 9973760 | tf_op jit(solution)/shard_map/dot_general | solution.py:262
  86.4 0.5 copy.74
  86.8 0.6 multiply_reduce_fusion
  87.5 0.1 copy.61
  87.6 0.1 copy.62
  87.7 1.9 %constant_dynamic-update-slice_fusion.6 = bf16[4096,512]{1,0:T(8,128)(2,1)} fusion(bf16[4096,512]{1,0:T(8,128)(2,1)} %get-tuple-element.38, bf16[512,512]{1,0:T(8,128)(2,1)} %collective-permute-done.3), kind=kLoop, calls=%fused_computation.43 | loop fusion | bytes 1048576
  89.6 3.3 %collective-permute-done.4 = bf16[512,512]{1,0:T(8,128)(2,1)} collective-permute-done((bf16[512,512]{1,0:T(8,128)(2,1)}, bf16[512,512]{1,0:T(8,128)(2,1)}, u32[]{:S(2)}, u32[]{:S(2)}) %collective-permute-start.4) | collective-permute-done | bytes 524320 | tf_op jit(solution)/shard_map/ppermute | solution.py:188
  93.0 1.4 collective-permute-done.6
  94.4 2.0 %broadcast_select_fusion = (bf16[512,512]{1,0:T(8,128)(2,1)S(1)}, bf16[4096,512]{1,0:T(8,128)(2,1)}) fusion(bf16[512,512]{1,0:T(8,128)(2,1)S(1)} %collective-permute-done.6, bf16[512,512]{1,0:T(8,128)(2,1)} %collective-permute-done.4, pred[]{:T(512)S(6)} %eq.40, bf16[4096,512]{1,0:T(8,128)(2,1)} %constant_dynamic-update-slice_fusion.6), kind=kLoop, calls=%fused_computation.27 | loop fusion | flops 262144 | bytes 2097153 | tf_op jit(solution)/shard_map/jit(_where)/select_n | solution.py:193
  96.4 0.2 collective-permute-start.8
  96.6 2.1 %collective-permute-start.5 = (bf16[512,512]{1,0:T(8,128)(2,1)}, bf16[512,512]{1,0:T(8,128)(2,1)S(1)}, u32[]{:S(2)}, u32[]{:S(2)}) collective-permute-start(bf16[512,512]{1,0:T(8,128)(2,1)} %collective-permute-done.4), channel_id=1, source_target_pairs={{0,4},{4,0},{8,12},{12,8},{16,20},{20,16},{24,28},{28,24},{1,5},{5... | collective-permute-start | bytes 1572872 | tf_op jit(solution)/shard_map/ppermute | solution.py:188
  98.8 0.8 multiply_multiply_fusion
  99.7 0.9 subtract_convert_fusion
  100.6 4.2 %collective-permute-done.8 = bf16[512,512]{1,0:T(8,128)(2,1)S(1)} collective-permute-done((bf16[512,512]{1,0:T(8,128)(2,1)S(1)}, bf16[512,512]{1,0:T(8,128)(2,1)S(1)}, u32[]{:S(2)}, u32[]{:S(2)}) %collective-permute-start.8) | collective-permute-done | bytes 524320 | tf_op jit(solution)/shard_map/ppermute | solution.py:194
  104.7 1.7 %collective-permute-start.9 = (bf16[512,512]{1,0:T(8,128)(2,1)S(1)}, bf16[512,512]{1,0:T(8,128)(2,1)S(1)}, u32[]{:S(2)}, u32[]{:S(2)}) collective-permute-start(bf16[512,512]{1,0:T(8,128)(2,1)S(1)} %collective-permute-done.8), channel_id=1, source_target_pairs={{0,4},{4,0},{8,12},{12,8},{16,20},{20,16},{24,28},{28,24},{1,5},{5... | collective-permute-start | bytes 1572872 | tf_op jit(solution)/shard_map/ppermute | solution.py:188
  106.4 0.6 pad_maximum_fusion.1
  107.0 1.3 copy.77
  108.3 0.8 constant_dynamic-update-slice_fusion.4
  109.1 0.8 constant_dynamic-update-slice_fusion.3
  110.0 0.8 constant_dynamic-update-slice_fusion.2
  110.8 0.8 constant_dynamic-update-slice_fusion.1
  111.6 0.8 constant_dynamic-update-slice_fusion.k_ref.v_ref
  112.5 1.2 dynamic-slice_bitcast_fusion.3
  113.8 0.2 copy.69
  114.0 0.9 copy.71
  114.9 0.2 copy.68
  115.0 0.9 copy.70
  115.9 38.1 %shard_map.112 = bf16[512,1024]{1,0:T(8,128)(2,1)} custom-call(s32[12]{0:T(128)} %reshape.205.meta_ref, s32[8]{0:T(128)} %copy-done, bf16[512,1024]{1,0:T(8,128)(2,1)} %bitcast.51, bf16[4096,512]{1,0:T(8,128)(2,1)} %constant_dynamic-update-slice_fusion.k_ref.v_ref, bf16[4096,512]{1,0:T(8,128)(2,1)} %constant_dynamic-update-slice_fusion.k_ref.v_ref, ...), custom_call_target="tpu_custom_call" | custom-call | flops 3221225472 | bytes 6291456 | tf_op jit(solution)/shard_map/pallas_call | solution.py:170
  (48 shorter events, 0.5 us)
Async XLA Ops:
  7.2 4.6 %copy-start.3 = (bf16[512,640]{1,0:T(8,128)(2,1)S(1)}, bf16[512,640]{1,0:T(8,128)(2,1)}, u32[]{:S(2)}) copy-start(bf16[512,640]{1,0:T(8,128)(2,1)} %param.9) | copy-start | bytes 1966084
  7.2 8.4 %copy-start.9 = (s32[8]{0:T(128)S(1)}, s32[8]{0:T(128)}, u32[]{:S(2)}) copy-start(s32[8]{0:T(128)} %param.16) | copy-start | bytes 100
  7.2 9.1 %copy-start.10 = (s32[32]{0:T(128)S(1)}, s32[32]{0:T(128)}, u32[]{:S(2)}) copy-start(s32[32]{0:T(128)} %param.17) | copy-start | bytes 388
  7.2 67.2 %all-gather.2.cloned.1.call-start = ((), (), s32[]{:S(2)}) async-start(), calls=%async_computation | async-start | bytes 8847360 | tf_op jit(solution)/shard_map/all_gather | solution.py:249
  11.7 17.4 %collective-permute-start = (bf16[512,640]{1,0:T(8,128)(2,1)S(1)}, bf16[512,640]{1,0:T(8,128)(2,1)S(1)}, u32[]{:S(2)}, u32[]{:S(2)}) collective-permute-start(bf16[512,640]{1,0:T(8,128)(2,1)S(1)} %copy-done.3), channel_id=1, source_target_pairs={{0,1},{1,2},{2,3},{3,0},{4,5},{5,6},{6,7},{7,4},{8,9},{9,10},{10,1... | collective-permute-start | bytes 1966088 | tf_op jit(solution)/shard_map/ppermute | solution.py:236
  13.1 55.5 %collective-permute-start.1 = (bf16[512,640]{1,0:T(8,128)(2,1)S(1)}, bf16[512,640]{1,0:T(8,128)(2,1)S(1)}, u32[]{:S(2)}, u32[]{:S(2)}) collective-permute-start(bf16[512,640]{1,0:T(8,128)(2,1)S(1)} %copy-done.3), channel_id=1, source_target_pairs={{0,2},{1,3},{2,0},{3,1},{4,6},{5,7},{6,4},{7,5},{8,10},{9,11},{10,... | collective-permute-start | bytes 1966088 | tf_op jit(solution)/shard_map/ppermute | solution.py:236
  14.2 57.4 %collective-permute-start.2 = (bf16[512,640]{1,0:T(8,128)(2,1)S(1)}, bf16[512,640]{1,0:T(8,128)(2,1)}, u32[]{:S(2)}, u32[]{:S(2)}) collective-permute-start(bf16[512,640]{1,0:T(8,128)(2,1)S(1)} %copy-done.3), channel_id=1, source_target_pairs={{0,3},{1,0},{2,1},{3,2},{4,7},{5,4},{6,5},{7,6},{8,11},{9,8},{10,9... | collective-permute-start | bytes 1966088 | tf_op jit(solution)/shard_map/ppermute | solution.py:236
  16.2 58.2 %copy-start = (s32[8]{0:T(128)}, s32[8]{0:T(128)S(1)}, u32[]{:S(2)}) copy-start(s32[8]{0:T(128)S(1)} %iota_xor_fusion.where_ref) | copy-start | bytes 100
  24.9 49.6 %copy-start.8 = (f32[2560]{0:T(1024)S(1)}, f32[2560]{0:T(1024)}, u32[]{:S(2)}) copy-start(f32[2560]{0:T(1024)} %param.10) | copy-start | bytes 30724
  29.1 39.5 %copy-start.4 = (bf16[512,640]{1,0:T(8,128)(2,1)}, bf16[512,640]{1,0:T(8,128)(2,1)S(1)}, u32[]{:S(2)}) copy-start(bf16[512,640]{1,0:T(8,128)(2,1)S(1)} %collective-permute-done) | copy-start | bytes 1966084
  68.6 0.9 copy-start.5
  74.4 3.6 %copy-start.6 = (f32[128]{0:T(128)S(1)}, f32[128]{0:T(128)}, u32[]{:S(2)}) copy-start(f32[128]{0:T(128)} %param.15) | copy-start | bytes 1540
  79.7 13.3 %collective-permute-start.4 = (bf16[512,512]{1,0:T(8,128)(2,1)}, bf16[512,512]{1,0:T(8,128)(2,1)}, u32[]{:S(2)}, u32[]{:S(2)}) collective-permute-start(bf16[512,512]{1,0:T(8,128)(2,1)} %get-tuple-element.37), channel_id=1, source_target_pairs={{0,8},{4,12},{8,0},{12,4},{16,24},{20,28},{24,16},{28,20},{1,9},{5... | collective-permute-start | bytes 1572872 | tf_op jit(solution)/shard_map/ppermute | solution.py:188
  79.9 7.8 %collective-permute-start.3 = (bf16[512,512]{1,0:T(8,128)(2,1)}, bf16[512,512]{1,0:T(8,128)(2,1)}, u32[]{:S(2)}, u32[]{:S(2)}) collective-permute-start(bf16[512,512]{1,0:T(8,128)(2,1)} %get-tuple-element.37), channel_id=1, source_target_pairs={{0,4},{4,0},{8,12},{12,8},{16,20},{20,16},{24,28},{28,24},{1,5},{5... | collective-permute-start | bytes 1572872 | tf_op jit(solution)/shard_map/ppermute | solution.py:188
  80.7 13.7 %collective-permute-start.6 = (bf16[512,512]{1,0:T(8,128)(2,1)}, bf16[512,512]{1,0:T(8,128)(2,1)S(1)}, u32[]{:S(2)}, u32[]{:S(2)}) collective-permute-start(bf16[512,512]{1,0:T(8,128)(2,1)} %get-tuple-element.37), channel_id=1, source_target_pairs={{0,16},{4,20},{8,24},{12,28},{16,0},{20,4},{24,8},{28,12},{1,17},{... | collective-permute-start | bytes 1572872 | tf_op jit(solution)/shard_map/ppermute | solution.py:188
  86.4 12.4 %copy-start.7 = (f32[128]{0:T(128)S(1)}, f32[128]{0:T(128)}, u32[]{:S(2)}) copy-start(f32[128]{0:T(128)} %param.14) | copy-start | bytes 1540
  87.5 12.2 %copy-start.1 = (f32[512,64]{1,0:T(8,128)S(1)}, f32[512,64]{1,0:T(8,128)}, u32[]{:S(2)}) copy-start(f32[512,64]{1,0:T(8,128)} %copy.63) | copy-start | bytes 393220
  87.5 12.2 %copy-start.2 = (f32[512,64]{1,0:T(8,128)S(1)}, f32[512,64]{1,0:T(8,128)}, u32[]{:S(2)}) copy-start(f32[512,64]{1,0:T(8,128)} %copy.64) | copy-start | bytes 393220
  96.4 8.3 %collective-permute-start.8 = (bf16[512,512]{1,0:T(8,128)(2,1)S(1)}, bf16[512,512]{1,0:T(8,128)(2,1)S(1)}, u32[]{:S(2)}, u32[]{:S(2)}) collective-permute-start(bf16[512,512]{1,0:T(8,128)(2,1)S(1)} %get-tuple-element.35), channel_id=1, source_target_pairs={{0,8},{4,20},{8,0},{12,28},{16,24},{20,4},{24,16},{28,12},{1,9},{5... | collective-permute-start | bytes 1572872 | tf_op jit(solution)/shard_map/ppermute | solution.py:194
  96.6 11.7 %collective-permute-start.5 = (bf16[512,512]{1,0:T(8,128)(2,1)}, bf16[512,512]{1,0:T(8,128)(2,1)S(1)}, u32[]{:S(2)}, u32[]{:S(2)}) collective-permute-start(bf16[512,512]{1,0:T(8,128)(2,1)} %collective-permute-done.4), channel_id=1, source_target_pairs={{0,4},{4,0},{8,12},{12,8},{16,20},{20,16},{24,28},{28,24},{1,5},{5... | collective-permute-start | bytes 1572872 | tf_op jit(solution)/shard_map/ppermute | solution.py:188
  99.6 10.4 %collective-permute-start.7 = (bf16[512,512]{1,0:T(8,128)(2,1)S(1)}, bf16[512,512]{1,0:T(8,128)(2,1)S(1)}, u32[]{:S(2)}, u32[]{:S(2)}) collective-permute-start(bf16[512,512]{1,0:T(8,128)(2,1)S(1)} %collective-permute-done.6), channel_id=1, source_target_pairs={{0,4},{4,0},{8,12},{12,8},{16,20},{20,16},{24,28},{28,24},{1,5},{5... | collective-permute-start | bytes 1572872 | tf_op jit(solution)/shard_map/ppermute | solution.py:188
  104.7 6.9 %collective-permute-start.9 = (bf16[512,512]{1,0:T(8,128)(2,1)S(1)}, bf16[512,512]{1,0:T(8,128)(2,1)S(1)}, u32[]{:S(2)}, u32[]{:S(2)}) collective-permute-start(bf16[512,512]{1,0:T(8,128)(2,1)S(1)} %collective-permute-done.8), channel_id=1, source_target_pairs={{0,4},{4,0},{8,12},{12,8},{16,20},{20,16},{24,28},{28,24},{1,5},{5... | collective-permute-start | bytes 1572872 | tf_op jit(solution)/shard_map/ppermute | solution.py:188
Sparse Core Ops, SparseCore 0:
  11.9 52.6 all-gather.1

commit v2 on v1

--- a/solution.py
+++ b/solution.py
@@ -243,12 +243,12 @@
         * lax.rsqrt(jnp.mean(widened * widened, axis=-1, keepdims=True) + epsilon)
         * norm_gain
     ).astype(jnp.bfloat16)
-    server_block = jnp.concatenate([query_weight, key_weight, value_weight], axis=1).astype(
-        jnp.bfloat16
-    )
-    full_block = lax.all_gather(server_block, "seq", axis=0, tiled=True)
+    kv_block = lax.all_gather(
+        jnp.concatenate([key_weight, value_weight], axis=1).astype(jnp.bfloat16), "seq", axis=0, tiled=True
+    )
+    q_block = lax.all_gather(query_weight.astype(jnp.bfloat16), "seq", axis=0, tiled=True)
     normed_perm = normed
-    projected_kv = jnp.dot(normed_perm, full_block[:, query_cols:], preferred_element_type=jnp.float32)
+    projected_kv = jnp.dot(normed_perm, kv_block, preferred_element_type=jnp.float32)
     slot_index = seq_rank * row_count + jnp.arange(row_count, dtype=jnp.int32)
     segment_id, position = position_of(slot_index, prompt_ends, lengths)
     key_rows = rotate(
@@ -259,7 +259,7 @@
     values = projected_kv[:, key_cols:].astype(jnp.bfloat16)
     local_kv = jnp.concatenate([key_rows, values], axis=1)
     both_piece, where = gather_rows(local_kv, chips)
-    projected_q = jnp.dot(normed_perm, full_block[:, :query_cols], preferred_element_type=jnp.float32)
+    projected_q = jnp.dot(normed_perm, q_block, preferred_element_type=jnp.float32)
     queries = rotate(
         head_norm(projected_q.reshape(row_count, query_cols // head_dim, head_dim), query_gain),
         position,

time: 158 us -> 186 us (1.18)
  the two profiles are of different devices: /device:TPU:15 before, /device:TPU:19 now
where the time goes in v2:
time: 186 us
  waiting for transfers between devices  72.1 us (39%)
  Pallas kernels  31.5 us (17%)
  local copies, waits for them, and re-layouts  24.9 us (13%)
  between operations  21.6 us (12%)
  other arithmetic  18.4 us (10%)
  matrix products  8.89 us (5%)
  starting transfers between devices  8.35 us (4%)
    ppermute x3, waiting for transfers between devices, shards(): pieces.append(lax.ppermute(hidden, 'tp', pairs))  55.5 us
    pallas_call x1, Pallas kernels, flash(): pl.pallas_call(kernel, grid_spec=grid_spec, out_shape=jax.ShapeDtypeStruc...  31.5 us
    unnamed x34, local copies, waits for them, and re-layouts  13.9 us
    ppermute x6, waiting for transfers between devices, swap(): return lax.ppermute(value, 'seq', [(i, i ^ bit) for i in range(seq_size)])  11.1 us
    ppermute x6, starting transfers between devices, swap(): return lax.ppermute(value, 'seq', [(i, i ^ bit) for i in range(seq_size)])  5.43 us
    dot_general x1, matrix products, shards(): jnp.dot(normed_perm, q_block, preferred_element_type=jnp.float32)  5.39 us
    ppermute x1, waiting for transfers between devices, gather_rows(): lax.ppermute(forward, 'seq', [(i, i ^ 2) if i % 2 == 0 else (i, i ^ 4) fo...  5.37 us
  transfers between devices with their start and end apart: 12, of which 7 were waited for; matrix products, arithmetic and copies ran while one was open for 20% of the time, Pallas kernels for 0%

profile of v2, /device:TPU:19, one launch (start us, length us, event | category | flops | bytes accessed | tf_op | source)
XLA Modules:
  0.0 185.7 jit_solution(14017188711431156079)
XLA Ops:
  7.2 1.0 convert.24
  8.3 1.0 convert.23
  9.3 0.8 pad_maximum_fusion.4
  10.1 2.3 %convert_element_type.32 = bf16[320,1024]{1,0:T(8,128)(2,1)} convert(f32[320,1024]{1,0:T(8,128)} %param.11) | non-fusion elementwise | flops 327680 | bytes 1966080 | tf_op jit(solution)/shard_map/convert_element_type | solution.py:249
  12.4 0.1 collective-permute-start.1
  12.5 2.4 %collective-permute-start.2 = (bf16[512,640]{1,0:T(8,128)(2,1)S(1)}, bf16[512,640]{1,0:T(8,128)(2,1)S(1)}, u32[]{:S(2)}, u32[]{:S(2)}) collective-permute-start(bf16[512,640]{1,0:T(8,128)(2,1)S(1)} %copy-done.4), channel_id=1, source_target_pairs={{0,3},{1,0},{2,1},{3,2},{4,7},{5,4},{6,5},{7,6},{8,11},{9,8},{10,9... | collective-permute-start | bytes 1966088 | tf_op jit(solution)/shard_map/ppermute | solution.py:236
  15.0 0.2 reduce-window.8
  15.3 0.5 multiply_cosine_fusion
  15.9 24.2 %collective-permute-done.1 = bf16[512,640]{1,0:T(8,128)(2,1)S(1)} collective-permute-done((bf16[512,640]{1,0:T(8,128)(2,1)S(1)}, bf16[512,640]{1,0:T(8,128)(2,1)S(1)}, u32[]{:S(2)}, u32[]{:S(2)}) %collective-permute-start.1) | collective-permute-done | bytes 655392 | tf_op jit(solution)/shard_map/ppermute | solution.py:236
  40.1 28.1 %collective-permute-done.2 = bf16[512,640]{1,0:T(8,128)(2,1)S(1)} collective-permute-done((bf16[512,640]{1,0:T(8,128)(2,1)S(1)}, bf16[512,640]{1,0:T(8,128)(2,1)S(1)}, u32[]{:S(2)}, u32[]{:S(2)}) %collective-permute-start.2) | collective-permute-done | bytes 655392 | tf_op jit(solution)/shard_map/ppermute | solution.py:236
  68.1 0.9 copy-done.6
  69.0 3.3 %collective-permute-done = bf16[512,640]{1,0:T(8,128)(2,1)} collective-permute-done((bf16[512,640]{1,0:T(8,128)(2,1)S(1)}, bf16[512,640]{1,0:T(8,128)(2,1)}, u32[]{:S(2)}, u32[]{:S(2)}) %collective-permute-start) | collective-permute-done | bytes 655392 | tf_op jit(solution)/shard_map/ppermute | solution.py:236
  72.3 1.9 %select_select_fusion.3 = (bf16[512,640]{1,0:T(8,128)(2,1)S(1)}, bf16[512,640]{1,0:T(8,128)(2,1)S(1)}, bf16[512,640]{1,0:T(8,128)(2,1)S(1)}, bf16[512,640]{1,0:T(8,128)(2,1)S(1)}) fusion(bf16[512,640]{1,0:T(8,128)(2,1)} %copy-done.5, bf16[512,640]{1,0:T(8,128)(2,1)} %copy-done.6, bf16[512,640]{1,0:T(8,128)(2,1)S(1)} %copy-done.4, ...), kind=kLoop, calls=%fused_computation.18 | loop fusion | flops 3932160 | bytes 5242892 | tf_op jit(solution)/shard_map/select_n | solution.py:238
  74.2 0.7 fusion
  75.0 3.5 %fusion.3 = f32[512,512]{0,1:T(8,128)S(1)} fusion(bf16[2560,512]{1,0:T(8,128)(2,1)} %all-gather.5.cloned.1.call-done, f32[2560]{0:T(1024)} %param.10, f32[512]{0:T(512)S(1)} %add_rsqrt_fusion.2, bf16[512,640]{1,0:T(8,128)(2,1)S(1)} %get-tuple-element.28, bf16[512,640]{1,0:T(8,128)(2,1)S(1)} %get-tuple-element.29, ...), kind=kOutput, calls=%fused_computation.14 | convolution fusion | flops 1356595200 | bytes 6303744 | tf_op jit(solution)/shard_map/dot_general | solution.py:251
  78.5 1.0 copy-done.1
  79.5 0.1 copy.73
  79.6 1.1 multiply_reduce_fusion.1
  80.8 1.2 multiply_multiply_fusion.1
  82.0 0.1 subtract_convert_fusion.1
  82.1 0.8 copy.72
  82.9 2.0 %pad_maximum_fusion.2 = (bf16[512,512]{1,0:T(8,128)(2,1)}, bf16[4096,512]{1,0:T(8,128)(2,1)}) fusion(bf16[512,256]{1,0:T(8,128)(2,1)S(1)} %copy.73, bf16[512,256]{1,0:T(8,128)(2,1)} %copy.72), kind=kLoop, calls=%fused_computation.19 | loop fusion | flops 1048575 | bytes 1572864 | tf_op jit(solution)/shard_map/concatenate | solution.py:260
  84.9 0.5 collective-permute-start.3
  85.5 1.2 collective-permute-start.6
  86.6 0.3 collective-permute-start.4
  86.9 0.2 select_reduce_fusion.1
  87.1 0.2 collective-permute-done.3
  87.4 1.9 %constant_dynamic-update-slice_fusion.6 = bf16[4096,512]{1,0:T(8,128)(2,1)} fusion(bf16[4096,512]{1,0:T(8,128)(2,1)} %get-tuple-element.38, bf16[512,512]{1,0:T(8,128)(2,1)} %collective-permute-done.3), kind=kLoop, calls=%fused_computation.40 | loop fusion | bytes 1048576
  89.2 10.0 %collective-permute-done.6 = bf16[512,512]{1,0:T(8,128)(2,1)S(1)} collective-permute-done((bf16[512,512]{1,0:T(8,128)(2,1)}, bf16[512,512]{1,0:T(8,128)(2,1)S(1)}, u32[]{:S(2)}, u32[]{:S(2)}) %collective-permute-start.6) | collective-permute-done | bytes 524320 | tf_op jit(solution)/shard_map/ppermute | solution.py:188
  99.3 0.9 collective-permute-done.4
  100.2 2.2 %broadcast_select_fusion = (bf16[512,512]{1,0:T(8,128)(2,1)}, bf16[4096,512]{1,0:T(8,128)(2,1)}) fusion(bf16[512,512]{1,0:T(8,128)(2,1)S(1)} %collective-permute-done.6, bf16[512,512]{1,0:T(8,128)(2,1)} %collective-permute-done.4, pred[]{:T(512)S(6)} %eq.40, bf16[4096,512]{1,0:T(8,128)(2,1)} %constant_dynamic-update-slice_fusion.6), kind=kLoop, calls=%fused_computation.23 | loop fusion | flops 262144 | bytes 2097153 | tf_op jit(solution)/shard_map/jit(_where)/select_n | solution.py:193
  102.3 0.3 collective-permute-start.8
  102.6 1.4 collective-permute-start.5
  104.1 0.6 gather_fusion
  104.7 0.1 slice.48
  104.8 0.1 slice.47
  104.9 0.1 slice.46
  105.0 0.6 fusion.11
  105.6 5.4 %collective-permute-done.8 = bf16[512,512]{1,0:T(8,128)(2,1)} collective-permute-done((bf16[512,512]{1,0:T(8,128)(2,1)}, bf16[512,512]{1,0:T(8,128)(2,1)}, u32[]{:S(2)}, u32[]{:S(2)}) %collective-permute-start.8) | collective-permute-done | bytes 524320 | tf_op jit(solution)/shard_map/ppermute | solution.py:194
  111.0 2.0 %collective-permute-start.9 = (bf16[512,512]{1,0:T(8,128)(2,1)}, bf16[512,512]{1,0:T(8,128)(2,1)}, u32[]{:S(2)}, u32[]{:S(2)}) collective-permute-start(bf16[512,512]{1,0:T(8,128)(2,1)} %collective-permute-done.8), channel_id=1, source_target_pairs={{0,4},{4,0},{8,12},{12,8},{16,20},{20,16},{24,28},{28,24},{1,5},{5... | collective-permute-start | bytes 1572872 | tf_op jit(solution)/shard_map/ppermute | solution.py:188
  113.0 0.8 copy.64
  113.8 0.8 copy.63
  119.6 0.6 reshape.205.meta_ref
  120.2 0.9 copy.67.rs_ref
  123.5 1.9 %constant_dynamic-update-slice_fusion.4 = bf16[4096,512]{1,0:T(8,128)(2,1)} fusion(bf16[4096,512]{1,0:T(8,128)(2,1)} %get-tuple-element.36, bf16[512,512]{1,0:T(8,128)(2,1)} %collective-permute-done.5), kind=kLoop, calls=%fused_computation.38 | loop fusion | bytes 1048576
  125.3 0.8 constant_dynamic-update-slice_fusion.3
  126.2 1.9 %constant_dynamic-update-slice_fusion.2 = bf16[4096,512]{1,0:T(8,128)(2,1)} fusion(bf16[4096,512]{1,0:T(8,128)(2,1)} %constant_dynamic-update-slice_fusion.3, bf16[512,512]{1,0:T(8,128)(2,1)} %collective-permute-done.7), kind=kLoop, calls=%fused_computation.36 | loop fusion | bytes 1048576
  128.1 1.9 %constant_dynamic-update-slice_fusion.1 = bf16[4096,512]{1,0:T(8,128)(2,1)} fusion(bf16[4096,512]{1,0:T(8,128)(2,1)} %constant_dynamic-update-slice_fusion.2, bf16[512,512]{1,0:T(8,128)(2,1)} %collective-permute-done.8), kind=kLoop, calls=%fused_computation.35 | loop fusion | bytes 1048576
  130.0 1.9 %constant_dynamic-update-slice_fusion.k_ref.v_ref = bf16[4096,512]{1,0:T(8,128)(2,1)} fusion(bf16[4096,512]{1,0:T(8,128)(2,1)} %constant_dynamic-update-slice_fusion.1, bf16[512,512]{1,0:T(8,128)(2,1)} %collective-permute-done.9), kind=kLoop, calls=%fused_computation.34 | loop fusion | bytes 1048576 | tf_op jit(solution)/shard_map/concatenate | solution.py:208
  131.9 1.2 dynamic-slice_bitcast_fusion.3
  133.3 0.7 fusion.10
  134.0 1.1 copy.68
  135.1 0.9 copy.70
  136.0 0.2 copy.69
  136.2 0.9 copy.71
  137.0 5.4 %convolution_bitcast_fusion = f32[64,8,8,128]{3,1,2,0:T(8,128)S(1)} fusion(bf16[2560,1024]{1,0:T(8,128)(2,1)} %all-gather.3.cloned.1.call-done, f32[2560]{0:T(1024)S(1)} %copy-done.9, f32[512]{0:T(512)S(1)} %add_rsqrt_fusion.2, bf16[512,640]{1,0:T(8,128)(2,1)S(1)} %get-tuple-element.28, bf16[512,640]{1,0:T(8,128)(2,1)S(1)} %get-tuple-element.29, ...), kind=kOutput, calls=%fused_computation.11 | convolution fusion | flops 2698772480 | bytes 9973760 | tf_op jit(solution)/shard_map/dot_general | solution.py:262
  142.4 0.5 copy.74
  142.9 0.6 multiply_reduce_fusion
  143.7 0.1 copy.62
  143.8 0.9 multiply_multiply_fusion
  144.7 0.9 subtract_convert_fusion
  145.5 0.6 pad_maximum_fusion.1
  146.1 1.3 copy.77
  147.4 31.5 %shard_map.112 = bf16[512,1024]{1,0:T(8,128)(2,1)} custom-call(s32[12]{0:T(128)} %reshape.205.meta_ref, s32[8]{0:T(128)} %copy-done, bf16[512,1024]{1,0:T(8,128)(2,1)} %bitcast.53, bf16[4096,512]{1,0:T(8,128)(2,1)} %constant_dynamic-update-slice_fusion.k_ref.v_ref, bf16[4096,512]{1,0:T(8,128)(2,1)} %constant_dynamic-update-slice_fusion.k_ref.v_ref, ...), custom_call_target="tpu_custom_call" | custom-call | flops 3221225472 | bytes 6291456 | tf_op jit(solution)/shard_map/pallas_call | solution.py:170
  (53 shorter events, 0.8 us)
Async XLA Ops:
  7.2 5.2 %copy-start.4 = (bf16[512,640]{1,0:T(8,128)(2,1)S(1)}, bf16[512,640]{1,0:T(8,128)(2,1)}, u32[]{:S(2)}) copy-start(bf16[512,640]{1,0:T(8,128)(2,1)} %param.9) | copy-start | bytes 1966084
  7.2 7.8 %copy-start.10 = (s32[8]{0:T(128)S(1)}, s32[8]{0:T(128)}, u32[]{:S(2)}) copy-start(s32[8]{0:T(128)} %param.16) | copy-start | bytes 100
  7.2 67.8 %all-gather.5.cloned.1.call-start = ((), (), s32[]{:S(2)}) async-start(), calls=%async_computation.1 | async-start | bytes 2949120 | tf_op jit(solution)/shard_map/all_gather | solution.py:246
  10.1 126.9 %all-gather.3.cloned.1.call-start = ((), (), s32[]{:S(2)}) async-start(), calls=%async_computation | async-start | bytes 5898240 | tf_op jit(solution)/shard_map/all_gather | solution.py:249
  12.4 27.6 %collective-permute-start.1 = (bf16[512,640]{1,0:T(8,128)(2,1)S(1)}, bf16[512,640]{1,0:T(8,128)(2,1)S(1)}, u32[]{:S(2)}, u32[]{:S(2)}) collective-permute-start(bf16[512,640]{1,0:T(8,128)(2,1)S(1)} %copy-done.4), channel_id=1, source_target_pairs={{0,2},{1,3},{2,0},{3,1},{4,6},{5,7},{6,4},{7,5},{8,10},{9,11},{10,... | collective-permute-start | bytes 1966088 | tf_op jit(solution)/shard_map/ppermute | solution.py:236
  12.5 55.6 %collective-permute-start.2 = (bf16[512,640]{1,0:T(8,128)(2,1)S(1)}, bf16[512,640]{1,0:T(8,128)(2,1)S(1)}, u32[]{:S(2)}, u32[]{:S(2)}) collective-permute-start(bf16[512,640]{1,0:T(8,128)(2,1)S(1)} %copy-done.4), channel_id=1, source_target_pairs={{0,3},{1,0},{2,1},{3,2},{4,7},{5,4},{6,5},{7,6},{8,11},{9,8},{10,9... | collective-permute-start | bytes 1966088 | tf_op jit(solution)/shard_map/ppermute | solution.py:236
  15.0 57.4 %collective-permute-start = (bf16[512,640]{1,0:T(8,128)(2,1)S(1)}, bf16[512,640]{1,0:T(8,128)(2,1)}, u32[]{:S(2)}, u32[]{:S(2)}) collective-permute-start(bf16[512,640]{1,0:T(8,128)(2,1)S(1)} %copy-done.4), channel_id=1, source_target_pairs={{0,1},{1,2},{2,3},{3,0},{4,5},{5,6},{6,7},{7,4},{8,9},{9,10},{10,1... | collective-permute-start | bytes 1966088 | tf_op jit(solution)/shard_map/ppermute | solution.py:236
  40.1 28.1 %copy-start.5 = (bf16[512,640]{1,0:T(8,128)(2,1)}, bf16[512,640]{1,0:T(8,128)(2,1)S(1)}, u32[]{:S(2)}) copy-start(bf16[512,640]{1,0:T(8,128)(2,1)S(1)} %collective-permute-done.1) | copy-start | bytes 1966084
  68.1 0.9 copy-start.6
  75.0 5.8 %copy-start.7 = (f32[128]{0:T(128)S(1)}, f32[128]{0:T(128)}, u32[]{:S(2)}) copy-start(f32[128]{0:T(128)} %param.15) | copy-start | bytes 1540
  78.5 1.0 copy-start.1
  79.5 7.5 %copy-start.11 = (s32[32]{0:T(128)S(1)}, s32[32]{0:T(128)}, u32[]{:S(2)}) copy-start(s32[32]{0:T(128)} %param.17) | copy-start | bytes 388
  84.9 2.4 %collective-permute-start.3 = (bf16[512,512]{1,0:T(8,128)(2,1)}, bf16[512,512]{1,0:T(8,128)(2,1)}, u32[]{:S(2)}, u32[]{:S(2)}) collective-permute-start(bf16[512,512]{1,0:T(8,128)(2,1)} %get-tuple-element.37), channel_id=1, source_target_pairs={{0,4},{4,0},{8,12},{12,8},{16,20},{20,16},{24,28},{28,24},{1,5},{5... | collective-permute-start | bytes 1572872 | tf_op jit(solution)/shard_map/ppermute | solution.py:188
  85.5 13.8 %collective-permute-start.6 = (bf16[512,512]{1,0:T(8,128)(2,1)}, bf16[512,512]{1,0:T(8,128)(2,1)S(1)}, u32[]{:S(2)}, u32[]{:S(2)}) collective-permute-start(bf16[512,512]{1,0:T(8,128)(2,1)} %get-tuple-element.37), channel_id=1, source_target_pairs={{0,16},{4,20},{8,24},{12,28},{16,0},{20,4},{24,8},{28,12},{1,17},{... | collective-permute-start | bytes 1572872 | tf_op jit(solution)/shard_map/ppermute | solution.py:188
  86.6 13.5 %collective-permute-start.4 = (bf16[512,512]{1,0:T(8,128)(2,1)}, bf16[512,512]{1,0:T(8,128)(2,1)}, u32[]{:S(2)}, u32[]{:S(2)}) collective-permute-start(bf16[512,512]{1,0:T(8,128)(2,1)} %get-tuple-element.37), channel_id=1, source_target_pairs={{0,8},{4,12},{8,0},{12,4},{16,24},{20,28},{24,16},{28,20},{1,9},{5... | collective-permute-start | bytes 1572872 | tf_op jit(solution)/shard_map/ppermute | solution.py:188
  102.3 8.6 %collective-permute-start.8 = (bf16[512,512]{1,0:T(8,128)(2,1)}, bf16[512,512]{1,0:T(8,128)(2,1)}, u32[]{:S(2)}, u32[]{:S(2)}) collective-permute-start(bf16[512,512]{1,0:T(8,128)(2,1)} %get-tuple-element.35), channel_id=1, source_target_pairs={{0,8},{4,20},{8,0},{12,28},{16,24},{20,4},{24,16},{28,12},{1,9},{5... | collective-permute-start | bytes 1572872 | tf_op jit(solution)/shard_map/ppermute | solution.py:194
  102.6 20.8 %collective-permute-start.5 = (bf16[512,512]{1,0:T(8,128)(2,1)}, bf16[512,512]{1,0:T(8,128)(2,1)}, u32[]{:S(2)}, u32[]{:S(2)}) collective-permute-start(bf16[512,512]{1,0:T(8,128)(2,1)} %collective-permute-done.4), channel_id=1, source_target_pairs={{0,4},{4,0},{8,12},{12,8},{16,20},{20,16},{24,28},{28,24},{1,5},{5... | collective-permute-start | bytes 1572872 | tf_op jit(solution)/shard_map/ppermute | solution.py:188
  104.1 29.2 %copy-start = (s32[8]{0:T(128)}, s32[8]{0:T(128)S(1)}, u32[]{:S(2)}) copy-start(s32[8]{0:T(128)S(1)} %iota_xor_fusion.where_ref) | copy-start | bytes 100
  104.7 21.5 %collective-permute-start.7 = (bf16[512,512]{1,0:T(8,128)(2,1)S(1)}, bf16[512,512]{1,0:T(8,128)(2,1)}, u32[]{:S(2)}, u32[]{:S(2)}) collective-permute-start(bf16[512,512]{1,0:T(8,128)(2,1)S(1)} %collective-permute-done.6), channel_id=1, source_target_pairs={{0,4},{4,0},{8,12},{12,8},{16,20},{20,16},{24,28},{28,24},{1,5},{5... | collective-permute-start | bytes 1572872 | tf_op jit(solution)/shard_map/ppermute | solution.py:188
  111.0 19.1 %collective-permute-start.9 = (bf16[512,512]{1,0:T(8,128)(2,1)}, bf16[512,512]{1,0:T(8,128)(2,1)}, u32[]{:S(2)}, u32[]{:S(2)}) collective-permute-start(bf16[512,512]{1,0:T(8,128)(2,1)} %collective-permute-done.8), channel_id=1, source_target_pairs={{0,4},{4,0},{8,12},{12,8},{16,20},{20,16},{24,28},{28,24},{1,5},{5... | collective-permute-start | bytes 1572872 | tf_op jit(solution)/shard_map/ppermute | solution.py:188
  126.2 10.8 %copy-start.9 = (f32[2560]{0:T(1024)S(1)}, f32[2560]{0:T(1024)}, u32[]{:S(2)}) copy-start(f32[2560]{0:T(1024)} %param.10) | copy-start | bytes 30724
  142.4 1.4 copy-start.8
  142.9 1.8 copy-start.2
  142.9 1.8 copy-start.3
Sparse Core Ops, SparseCore 0:
  10.2 31.4 all-gather.4
  43.5 40.9 all-gather.2
